TPU v7x, 128 devices: a whole 4x4x4 slice. The times are simulated.
128 devices in a mesh: scen: 8 (over y, x_lo), gx: 4 (over x_hi, core), gy: 4 (over z).
Axes of the slice: x: 4 (x_hi: 2, x_lo: 2; x = x_hi * 2 + x_lo), y: 4, z: 4, core: 2. Of those that a mesh axis runs over, the one named last changes fastest.
Arguments:
- source: float32 [8, 32, 1024, 1024], P('scen', None, 'gx', 'gy'), may hold values from 0.2 to 3
- obstacle: int32 [32, 1024, 1024], P(None, 'gx', 'gy'), may hold values 0 or 1
- sector: int32 [8], P('scen'), may hold values from 0 to 15
- freq_class: int32 [8], P('scen'), may hold values from 0 to 4
Outputs:
- risk: float32 [16, 1024, 1024], P('scen', 'gx', 'gy')
All inputs are finite; a program needn't handle non-finite values. No bound on the sum of `obstacle` on one device may be relied on, other than what follows from the above.
Results may differ from a plain program's by a relative error of at most 0.00002.
Values sent between devices are 32-bit elements; how exact they have to be, the bound alone decides.
No kernel may reach another device: no remote copies, remote signals or barrier semaphores. Data moves between devices by JAX's collectives and lax.ppermute only.
A program may use at most 256 MiB of HBM per device.

v0:
```python
import math
import jax
import jax.numpy as jnp
from jax import lax
from jax.sharding import PartitionSpec as P

STEPS = 4
RZ = 16
wind_speed = 0.4
diffusion = 0.05
settling = 0.1
probit_a = 3.0
probit_b = 1.0
load_eps = 0.01
freq_rate = 0.7


def with_halo(block, sides, width):
    for axis, dim in sides:
        count = lax.axis_size(axis)
        forward = [(i, i + 1) for i in range(count - 1)]
        backward = [(target, source) for source, target in forward]
        low = lax.ppermute(
            lax.slice_in_dim(block, block.shape[dim] - width, None, axis=dim), axis, forward
        )
        high = lax.ppermute(lax.slice_in_dim(block, 0, width, axis=dim), axis, backward)
        block = jnp.concatenate([low, block, high], axis=dim)
    return block


def wind_components(sector_id):
    heading = sector_id.astype(jnp.float32) * (2.0 * math.pi / 16.0)
    return (wind_speed * jnp.cos(heading), wind_speed * jnp.sin(heading))


def advance(padded, open_cells, courant_x, courant_y):
    centre = padded[:, 1:-1, 1:-1]
    west_side = padded[:, :-2, 1:-1]
    east_side = padded[:, 2:, 1:-1]
    south_side = padded[:, 1:-1, :-2]
    north_side = padded[:, 1:-1, 2:]
    zero_plane = jnp.zeros_like(centre[:1])
    upper_cell = jnp.concatenate([centre[1:], zero_plane], 0)
    lower_cell = jnp.concatenate([centre[:1], centre[:-1]], 0)
    falling = jnp.concatenate([zero_plane, centre[1:]], 0)
    advect = jnp.maximum(courant_x, 0.0) * (centre - west_side) + jnp.minimum(courant_x, 0.0) * (
        east_side - centre
    )
    advect = (
        advect
        + jnp.maximum(courant_y, 0.0) * (centre - south_side)
        + jnp.minimum(courant_y, 0.0) * (north_side - centre)
    )
    spread = (
        west_side + east_side + south_side + north_side + upper_cell + lower_cell - 6.0 * centre
    )
    return (centre - advect + diffusion * spread + settling * (upper_cell - falling)) * open_cells


def lethality(toxic_load):
    probit = probit_a + probit_b * jnp.log(toxic_load + load_eps)
    return 0.5 * (1.0 + lax.erf((probit - 5.0) / math.sqrt(2.0)))


def on_device(source, obstacle, sector, freq_class):
    open_cells = (1 - obstacle).astype(jnp.float32)
    courant_x, courant_y = wind_components(sector[0])
    weight = jnp.exp(-freq_rate * freq_class[0].astype(jnp.float32))
    current = source[0] * open_cells
    toxic_load = jnp.zeros_like(current)
    for step_index in range(STEPS):
        padded = with_halo(current, (("gx", 1), ("gy", 2)), 1)
        current = advance(padded, open_cells, courant_x, courant_y)
        toxic_load = toxic_load + current * current
    weighted = weight * lethality(toxic_load[:RZ])
    summed = lax.psum(weighted, "scen")
    share = RZ // lax.axis_size("scen")
    return lax.dynamic_slice_in_dim(summed, lax.axis_index("scen") * share, share, 0)


def solution(mesh):
    in_specs = (P("scen", None, "gx", "gy"), P(None, "gx", "gy"), P("scen"), P("scen"))
    out_specs = P("scen", "gx", "gy")
    return jax.shard_map(
        on_device, mesh=mesh, in_specs=in_specs, out_specs=out_specs, check_vma=False
    )
```

profile of v0, /device:TPU:1, one launch (start us, length us, event | category | flops | bytes accessed | tf_op | source)
XLA Modules:
  0.0 627.8 jit_solution(8884289977543023363)
XLA Ops:
  6.5 16.5 %bitcast_multiply_fusion = f32[32,256,256]{2,0,1:T(8,128)S(1)} fusion(f32[1,32,256,256]{3,2,1,0:T(8,128)} %param.4, s32[32,256,256]{2,1,0:T(8,128)} %param.5), kind=kLoop, calls=%fused_computation.103 | loop fusion | flops 6291456 | bytes 25165824 | tf_op jit(solution)/shard_map/mul | solution.py:69
  23.0 6.0 collective-permute-start
  29.1 1.9 collective-permute-start.1
  31.0 4.8 collective-permute-done.1
  35.8 0.9 pad_maximum_fusion
  36.7 5.0 fusion.83
  41.7 3.7 copy.10
  45.4 3.5 collective-permute-start.2
  49.0 3.7 copy.12
  52.7 1.5 collective-permute-start.3
  54.2 13.4 %fusion.90 = (f32[31,256,256]{2,0,1:T(8,128)}, f32[31,256,256]{2,0,1:T(8,128)}) fusion(f32[32,256,256]{2,0,1:T(8,128)} %copy-done), kind=kLoop, calls=%fused_computation.136 | loop fusion | bytes 32505856 | tf_op jit(solution)/shard_map/slice | solution.py:43
  68.4 1.7 slice.205
  70.2 3.9 copy.11
  74.1 3.9 copy.13
  78.0 39.9 %fusion.59 = f32[32,256,256]{2,0,1:T(8,128)} fusion(f32[32,1,256]{2,0,1:T(8,128)S(1)} %collective-permute-done.1, f32[32,256,256]{2,0,1:T(8,128)} %copy-done, f32[32,1,256]{2,0,1:T(8,128)S(1)} %collective-permute-done, f32[31,256,256]{2,0,1:T(8,128)} %get-tuple-element.26, f32[1,256,256]{2,0,1:T(1,128)S(1)} %slice.205, ...), kind=kLoop, calls=%fused_computation.94 | loop fusion | flops 75497472 | bytes 41812496 | tf_op jit(solution)/shard_map/mul | solution.py:57
  117.9 0.8 fusion.89
  118.7 2.2 collective-permute-start.4
  120.9 2.1 collective-permute-start.5
  123.0 4.6 collective-permute-done.5
  127.6 4.0 pad_maximum_fusion.1
  131.6 4.8 fusion.82
  136.4 3.7 copy.14
  140.2 4.7 collective-permute-start.6
  144.8 3.7 copy.16
  148.6 1.3 collective-permute-start.7
  149.9 13.5 %fusion.88 = (f32[31,256,256]{2,0,1:T(8,128)}, f32[31,256,256]{2,0,1:T(8,128)}) fusion(f32[32,256,256]{2,0,1:T(8,128)} %fusion.59), kind=kLoop, calls=%fused_computation.134 | loop fusion | bytes 32505856 | tf_op jit(solution)/shard_map/slice | solution.py:43
  163.4 1.7 slice.212
  165.1 3.9 copy.15
  169.0 3.9 copy.17
  172.9 39.3 %fusion.41 = f32[32,256,256]{2,0,1:T(8,128)} fusion(f32[32,1,256]{2,0,1:T(8,128)S(1)} %collective-permute-done.5, f32[32,256,256]{2,0,1:T(8,128)} %fusion.59, f32[32,1,256]{2,0,1:T(8,128)S(1)} %collective-permute-done.4, f32[31,256,256]{2,0,1:T(8,128)} %get-tuple-element.22, f32[1,256,256]{2,0,1:T(1,128)S(1)} %slice.212, ...), kind=kLoop, calls=%fused_computation.68 | loop fusion | flops 75497472 | bytes 41812496 | tf_op jit(solution)/shard_map/mul | solution.py:57
  212.2 0.8 fusion.87
  213.0 2.2 collective-permute-start.8
  215.2 2.3 collective-permute-start.9
  217.5 4.4 collective-permute-done.9
  221.9 4.0 pad_maximum_fusion.2
  225.9 4.8 fusion.81
  230.8 3.7 copy.18
  234.5 4.3 collective-permute-start.10
  238.8 3.7 copy.20
  242.5 1.3 collective-permute-start.11
  243.8 13.4 %fusion.86 = (f32[31,256,256]{2,0,1:T(8,128)}, f32[31,256,256]{2,0,1:T(8,128)}) fusion(f32[32,256,256]{2,0,1:T(8,128)} %fusion.41), kind=kLoop, calls=%fused_computation.132 | loop fusion | bytes 32505856 | tf_op jit(solution)/shard_map/slice | solution.py:43
  257.2 1.7 slice.219
  258.9 3.8 copy.19
  262.8 3.8 copy.21
  266.6 40.3 %fusion.23 = f32[32,256,256]{2,0,1:T(8,128)} fusion(f32[32,1,256]{2,0,1:T(8,128)S(1)} %collective-permute-done.9, f32[32,256,256]{2,0,1:T(8,128)} %fusion.41, f32[32,1,256]{2,0,1:T(8,128)S(1)} %collective-permute-done.8, f32[31,256,256]{2,0,1:T(8,128)} %get-tuple-element.18, f32[1,256,256]{2,0,1:T(1,128)S(1)} %slice.219, ...), kind=kLoop, calls=%fused_computation.42 | loop fusion | flops 75497472 | bytes 41812496 | tf_op jit(solution)/shard_map/mul | solution.py:57
  307.7 2.2 collective-permute-start.12
  309.9 2.7 collective-permute-start.13
  312.6 11.7 %fusion.67 = f32[32,256,256]{2,0,1:T(8,128)} fusion(s32[32,256,256]{2,1,0:T(8,128)} %param.5), kind=kLoop, calls=%fused_computation.105 | loop fusion | flops 4194304 | bytes 16777216 | tf_op jit(solution)/shard_map/convert_element_type | solution.py:66
  325.1 1.8 pad_maximum_fusion.3
  326.9 4.9 fusion.80
  331.8 3.7 copy.22
  335.5 4.2 collective-permute-start.14
  339.7 3.7 copy.24
  343.5 1.5 collective-permute-start.15
  345.0 13.4 %fusion.84 = (f32[31,256,256]{2,0,1:T(8,128)}, f32[31,256,256]{2,0,1:T(8,128)}) fusion(f32[32,256,256]{2,0,1:T(8,128)} %fusion.23), kind=kLoop, calls=%fused_computation.130 | loop fusion | bytes 32505856 | tf_op jit(solution)/shard_map/slice | solution.py:44
  358.5 1.7 slice.226
  360.2 3.8 copy.23
  364.0 3.9 copy.25
  367.9 23.8 %fusion.10 = f32[32,256,256]{2,0,1:T(8,128)} fusion(f32[32,256,256]{2,0,1:T(8,128)} %fusion.23, f32[32,1,256]{2,0,1:T(8,128)S(1)} %collective-permute-done.13, f32[32,1,256]{2,0,1:T(8,128)S(1)} %collective-permute-done.12, f32[32,258,1]{2,0,1:T(8,128)} %copy.23, f32[32,258,1]{2,0,1:T(8,128)} %copy.25, f32[]{:T(128)} %bitcast.4, f32[]{:T(128)} %bitcast.3, ...), kind=kLoop, calls=%fused_computation.21 | loop fusion | flops 39845888 | bytes 16908816 | tf_op jit(solution)/shard_map/add | solution.py:50
  391.8 27.2 %fusion.6 = f32[32,256,256]{2,0,1:T(8,128)} fusion(f32[32,1,256]{2,0,1:T(8,128)S(1)} %collective-permute-done.13, f32[32,256,256]{2,0,1:T(8,128)} %fusion.23, f32[32,1,256]{2,0,1:T(8,128)S(1)} %collective-permute-done.12, f32[31,256,256]{2,0,1:T(8,128)} %get-tuple-element.13, f32[1,256,256]{2,0,1:T(1,128)S(1)} %slice.226, ...), kind=kLoop, calls=%fused_computation.17 | loop fusion | flops 33554432 | bytes 33423872 | tf_op jit(solution)/shard_map/sub | solution.py:55
  419.1 13.3 %add_multiply_fusion = f32[16,256,256]{2,0,1:T(8,128)} fusion(f32[32,256,256]{2,0,1:T(8,128)} %fusion.67, f32[31,256,256]{2,0,1:T(8,128)} %get-tuple-element.14, f32[32,256,256]{2,0,1:T(8,128)} %fusion.6, f32[32,256,256]{2,0,1:T(8,128)} %fusion.10, f32[32,256,256]{2,0,1:T(8,128)S(1)} %bitcast.10, f32[32,256,256]{2,0,1:T(8,128)} %fusion.41, ...), kind=kLoop, calls=%fused_computation.124 | loop fusion | flops 19922944 | bytes 37486596 | tf_op jit(solution)/shard_map/mul | solution.py:75
  432.4 185.5 %all-reduce.10.cloned.1.call-done = f32[16,256,256]{2,0,1:T(8,128)} async-done(((f32[16,256,256]{2,0,1:T(8,128)}), f32[16,256,256]{2,0,1:T(8,128)}) %all-reduce.10.cloned.1.call-update) | async-done | bytes 4194320 | tf_op jit(solution)/shard_map/psum | solution.py:76
  617.9 1.8 constant_dynamic-slice_fusion
  619.7 0.8 copy.26
  (34 shorter events, 0.9 us)
Async XLA Ops:
  6.5 611.4 %all-reduce.10.cloned.1.call-start = ((), (), s32[]{:S(2)}) async-start(), calls=%async_computation | async-start | bytes 8388608 | tf_op jit(solution)/shard_map/psum | solution.py:76
  23.0 12.8 %copy-start = (f32[32,256,256]{2,0,1:T(8,128)}, f32[32,256,256]{2,0,1:T(8,128)S(1)}, u32[]{:S(2)}) copy-start(f32[32,256,256]{2,0,1:T(8,128)S(1)} %bitcast_multiply_fusion) | copy-start | bytes 25165828
  23.0 8.0 %collective-permute-start = (f32[32,1,256]{2,0,1:T(8,128)S(1)}, f32[32,1,256]{2,0,1:T(8,128)S(1)}, u32[]{:S(2)}, u32[]{:S(2)}) collective-permute-start(f32[32,1,256]{2,0,1:T(8,128)S(1)} %get-tuple-element.27), channel_id=1, source_target_pairs={{0,4},{4,8},{8,12},{1,5},{5,9},{9,13},{2,6},{6,10},{10,14},{3,7},{... | collective-permute-start | bytes 98312 | tf_op jit(solution)/shard_map/ppermute | solution.py:23
  29.1 6.7 %collective-permute-start.1 = (f32[32,1,256]{2,0,1:T(8,128)S(1)}, f32[32,1,256]{2,0,1:T(8,128)S(1)}, u32[]{:S(2)}, u32[]{:S(2)}) collective-permute-start(f32[32,1,256]{2,0,1:T(8,128)S(1)} %get-tuple-element.28), channel_id=1, source_target_pairs={{4,0},{8,4},{12,8},{5,1},{9,5},{13,9},{6,2},{10,6},{14,10},{7,3},{... | collective-permute-start | bytes 98312 | tf_op jit(solution)/shard_map/ppermute | solution.py:26
  45.4 24.7 %collective-permute-start.2 = (f32[32,258,1]{1,0,2:T(8,128)S(1)}, f32[32,258,1]{1,0,2:T(8,128)S(1)}, u32[]{:S(2)}, u32[]{:S(2)}) collective-permute-start(f32[32,258,1]{1,0,2:T(8,128)S(1)} %copy.10), channel_id=1, source_target_pairs={{0,1},{1,2},{2,3},{4,5},{5,6},{6,7},{8,9},{9,10},{10,11},{12,13},{... | collective-permute-start | bytes 99080 | tf_op jit(solution)/shard_map/ppermute | solution.py:23
  52.7 21.4 %collective-permute-start.3 = (f32[32,258,1]{1,0,2:T(8,128)S(1)}, f32[32,258,1]{1,0,2:T(8,128)S(1)}, u32[]{:S(2)}, u32[]{:S(2)}) collective-permute-start(f32[32,258,1]{1,0,2:T(8,128)S(1)} %copy.12), channel_id=1, source_target_pairs={{1,0},{2,1},{3,2},{5,4},{6,5},{7,6},{9,8},{10,9},{11,10},{13,12},{... | collective-permute-start | bytes 99080 | tf_op jit(solution)/shard_map/ppermute | solution.py:26
  118.7 4.3 collective-permute-start.4
  120.9 6.7 %collective-permute-start.5 = (f32[32,1,256]{2,0,1:T(8,128)S(1)}, f32[32,1,256]{2,0,1:T(8,128)S(1)}, u32[]{:S(2)}, u32[]{:S(2)}) collective-permute-start(f32[32,1,256]{2,0,1:T(8,128)S(1)} %get-tuple-element.24), channel_id=1, source_target_pairs={{4,0},{8,4},{12,8},{5,1},{9,5},{13,9},{6,2},{10,6},{14,10},{7,3},{... | collective-permute-start | bytes 98312 | tf_op jit(solution)/shard_map/ppermute | solution.py:26
  140.2 24.9 %collective-permute-start.6 = (f32[32,258,1]{1,0,2:T(8,128)S(1)}, f32[32,258,1]{1,0,2:T(8,128)S(1)}, u32[]{:S(2)}, u32[]{:S(2)}) collective-permute-start(f32[32,258,1]{1,0,2:T(8,128)S(1)} %copy.14), channel_id=1, source_target_pairs={{0,1},{1,2},{2,3},{4,5},{5,6},{6,7},{8,9},{9,10},{10,11},{12,13},{... | collective-permute-start | bytes 99080 | tf_op jit(solution)/shard_map/ppermute | solution.py:23
  148.6 20.4 %collective-permute-start.7 = (f32[32,258,1]{1,0,2:T(8,128)S(1)}, f32[32,258,1]{1,0,2:T(8,128)S(1)}, u32[]{:S(2)}, u32[]{:S(2)}) collective-permute-start(f32[32,258,1]{1,0,2:T(8,128)S(1)} %copy.16), channel_id=1, source_target_pairs={{1,0},{2,1},{3,2},{5,4},{6,5},{7,6},{9,8},{10,9},{11,10},{13,12},{... | collective-permute-start | bytes 99080 | tf_op jit(solution)/shard_map/ppermute | solution.py:26
  213.0 4.5 collective-permute-start.8
  215.2 6.7 %collective-permute-start.9 = (f32[32,1,256]{2,0,1:T(8,128)S(1)}, f32[32,1,256]{2,0,1:T(8,128)S(1)}, u32[]{:S(2)}, u32[]{:S(2)}) collective-permute-start(f32[32,1,256]{2,0,1:T(8,128)S(1)} %get-tuple-element.20), channel_id=1, source_target_pairs={{4,0},{8,4},{12,8},{5,1},{9,5},{13,9},{6,2},{10,6},{14,10},{7,3},{... | collective-permute-start | bytes 98312 | tf_op jit(solution)/shard_map/ppermute | solution.py:26
  234.5 24.4 %collective-permute-start.10 = (f32[32,258,1]{1,0,2:T(8,128)S(1)}, f32[32,258,1]{1,0,2:T(8,128)S(1)}, u32[]{:S(2)}, u32[]{:S(2)}) collective-permute-start(f32[32,258,1]{1,0,2:T(8,128)S(1)} %copy.18), channel_id=1, source_target_pairs={{0,1},{1,2},{2,3},{4,5},{5,6},{6,7},{8,9},{9,10},{10,11},{12,13},{... | collective-permute-start | bytes 99080 | tf_op jit(solution)/shard_map/ppermute | solution.py:23
  242.5 20.2 %collective-permute-start.11 = (f32[32,258,1]{1,0,2:T(8,128)S(1)}, f32[32,258,1]{1,0,2:T(8,128)S(1)}, u32[]{:S(2)}, u32[]{:S(2)}) collective-permute-start(f32[32,258,1]{1,0,2:T(8,128)S(1)} %copy.20), channel_id=1, source_target_pairs={{1,0},{2,1},{3,2},{5,4},{6,5},{7,6},{9,8},{10,9},{11,10},{13,12},{... | collective-permute-start | bytes 99080 | tf_op jit(solution)/shard_map/ppermute | solution.py:26
  307.7 17.4 %collective-permute-start.12 = (f32[32,1,256]{2,0,1:T(8,128)S(1)}, f32[32,1,256]{2,0,1:T(8,128)S(1)}, u32[]{:S(2)}, u32[]{:S(2)}) collective-permute-start(f32[32,1,256]{2,0,1:T(8,128)S(1)} %get-tuple-element.15), channel_id=1, source_target_pairs={{0,4},{4,8},{8,12},{1,5},{5,9},{9,13},{2,6},{6,10},{10,14},{3,7},{... | collective-permute-start | bytes 98312 | tf_op jit(solution)/shard_map/ppermute | solution.py:23
  309.9 15.2 %slice-start = ((s8[8388608]{0:T(1024)(128)(4,1)}), s8[4194304]{0:T(1024)(128)(4,1)S(1)}, s32[]{:S(2)}) async-start(s8[8388608]{0:T(1024)(128)(4,1)} %bitcast.7), calls=%async_computation.1 | async-start | bytes 8388608
  309.9 15.2 %slice-start.1 = ((s8[8388608]{0:T(1024)(128)(4,1)}), s8[4194304]{0:T(1024)(128)(4,1)S(1)}, s32[]{:S(2)}) async-start(s8[8388608]{0:T(1024)(128)(4,1)} %bitcast.7), calls=%async_computation.2 | async-start | bytes 8388608
  309.9 15.2 %collective-permute-start.13 = (f32[32,1,256]{2,0,1:T(8,128)S(1)}, f32[32,1,256]{2,0,1:T(8,128)S(1)}, u32[]{:S(2)}, u32[]{:S(2)}) collective-permute-start(f32[32,1,256]{2,0,1:T(8,128)S(1)} %get-tuple-element.16), channel_id=1, source_target_pairs={{4,0},{8,4},{12,8},{5,1},{9,5},{13,9},{6,2},{10,6},{14,10},{7,3},{... | collective-permute-start | bytes 98312 | tf_op jit(solution)/shard_map/ppermute | solution.py:26
  335.5 24.7 %collective-permute-start.14 = (f32[32,258,1]{1,0,2:T(8,128)S(1)}, f32[32,258,1]{1,0,2:T(8,128)S(1)}, u32[]{:S(2)}, u32[]{:S(2)}) collective-permute-start(f32[32,258,1]{1,0,2:T(8,128)S(1)} %copy.22), channel_id=1, source_target_pairs={{0,1},{1,2},{2,3},{4,5},{5,6},{6,7},{8,9},{9,10},{10,11},{12,13},{... | collective-permute-start | bytes 99080 | tf_op jit(solution)/shard_map/ppermute | solution.py:23
  343.5 20.5 %collective-permute-start.15 = (f32[32,258,1]{1,0,2:T(8,128)S(1)}, f32[32,258,1]{1,0,2:T(8,128)S(1)}, u32[]{:S(2)}, u32[]{:S(2)}) collective-permute-start(f32[32,258,1]{1,0,2:T(8,128)S(1)} %copy.24), channel_id=1, source_target_pairs={{1,0},{2,1},{3,2},{5,4},{6,5},{7,6},{9,8},{10,9},{11,10},{13,12},{... | collective-permute-start | bytes 99080 | tf_op jit(solution)/shard_map/ppermute | solution.py:26
  364.0 27.8 %slice-start.4 = ((s8[4227072]{0:T(1024)(128)(4,1)}), s8[32768]{0:T(1024)(128)(4,1)S(1)}, s32[]{:S(2)}) async-start(s8[4227072]{0:T(1024)(128)(4,1)} %bitcast.11), calls=%async_computation.5 | async-start | bytes 65536
  367.9 23.8 %slice-start.5 = ((s8[4227072]{0:T(1024)(128)(4,1)}), s8[4194304]{0:T(1024)(128)(4,1)S(1)}, s32[]{:S(2)}) async-start(s8[4227072]{0:T(1024)(128)(4,1)} %bitcast.11), calls=%async_computation.6 | async-start | bytes 8388608
  367.9 51.1 %slice-start.2 = ((s8[8388608]{0:T(1024)(128)(4,1)}), s8[4194304]{0:T(1024)(128)(4,1)S(1)}, s32[]{:S(2)}) async-start(s8[8388608]{0:T(1024)(128)(4,1)} %bitcast.9), calls=%async_computation.3 | async-start | bytes 8388608
  391.8 27.3 %slice-start.3 = ((s8[8388608]{0:T(1024)(128)(4,1)}), s8[4194304]{0:T(1024)(128)(4,1)S(1)}, s32[]{:S(2)}) async-start(s8[8388608]{0:T(1024)(128)(4,1)} %bitcast.9), calls=%async_computation.4 | async-start | bytes 8388608
Sparse Core Ops, SparseCore 0:
  432.5 185.3 all-reduce.9
where the time goes:
time: 637 us; the launch traced here: 628 us
  other arithmetic  223 us (35%)
  waiting for transfers between devices  199 us (31%)
  local copies, waits for them, and re-layouts  146 us (23%)
  starting transfers between devices  44 us (7%)
  between operations  15.8 us (2%)
    psum x1, waiting for transfers between devices, on_device(): summed = lax.psum(weighted, 'scen')  186 us
    mul x3, other arithmetic, advance(): (centre - advect + diffusion * spread + settling * (upper_cell - falling)...  120 us
    slice x3, local copies, waits for them, and re-layouts, advance(): upper_cell = jnp.concatenate([centre[1:], zero_plane], 0)  40.2 us
    slice x11, local copies, waits for them, and re-layouts, with_halo(): lax.slice_in_dim(block, block.shape[dim] - width, None, axis=dim)  31.9 us
    ppermute x8, starting transfers between devices, with_halo(): lax.ppermute(lax.slice_in_dim(block, block.shape[dim] - width, None, axis...  29.2 us
    sub x1, other arithmetic, advance(): west_side + east_side + south_side + north_side + upper_cell + lower_cell  27.2 us
    add x1, other arithmetic, advance(): advect + jnp.maximum(courant_y, 0.0) * (centre - south_side)  23.8 us
    slice x5, local copies, waits for them, and re-layouts, advance(): lower_cell = jnp.concatenate([centre[:1], centre[:-1]], 0)  20.3 us
  transfers between devices with their start and end apart: 17, of which 4 were waited for; matrix products, arithmetic and copies ran while one was open for 16% of the time, Pallas kernels for 0%

commit v1 on v0

--- a/solution.py
+++ b/solution.py
@@ -13,6 +13,11 @@
 probit_b = 1.0
 load_eps = 0.01
 freq_rate = 0.7
+
+
+def prepare_pools_on(t0):
+    now = jnp.sum(lax.all_gather(t0, "scen"), axis=0)
+    return now
 
 
 def with_halo(block, sides, width):
@@ -73,7 +78,7 @@
         current = advance(padded, open_cells, courant_x, courant_y)
         toxic_load = toxic_load + current * current
     weighted = weight * lethality(toxic_load[:RZ])
-    summed = lax.psum(weighted, "scen")
+    summed = prepare_pools_on(weighted)
     share = RZ // lax.axis_size("scen")
     return lax.dynamic_slice_in_dim(summed, lax.axis_index("scen") * share, share, 0)
 

time: 637 us -> 1110 us (1.74)
  waiting for transfers between devices: 199 us -> 657 us
  other arithmetic: 223 us -> 235 us
    all_gather x0 -> x1, waiting for transfers between devices: none -> 643 us  [prepare_pools_on(): now = jnp.sum(lax.all_gather(t0, 'scen'), axis=0)]
    psum x1 -> x0, waiting for transfers between devices: 186 us -> none  [on_device(): summed = lax.psum(weighted, 'scen')]
    reduce_sum x0 -> x1, other arithmetic: none -> 14.4 us  [prepare_pools_on(): now = jnp.sum(lax.all_gather(t0, 'scen'), axis=0)]
  transfers between devices with their start and end apart: 17 -> 17, of which waited for: 4 -> 4; matrix products, arithmetic and copies ran while one was open for 16% -> 9% of each run, Pallas kernels for 0% -> 0%
where the time goes in v1:
time: 1110 us; the launch traced here: 1100 us
  waiting for transfers between devices  657 us (59%)
  other arithmetic  235 us (21%)
  local copies, waits for them, and re-layouts  150 us (14%)
  starting transfers between devices  44 us (4%)
  between operations  15.8 us (1%)
    all_gather x1, waiting for transfers between devices, prepare_pools_on(): now = jnp.sum(lax.all_gather(t0, 'scen'), axis=0)  643 us
    mul x3, other arithmetic, advance(): (centre - advect + diffusion * spread + settling * (upper_cell - falling)...  120 us
    slice x3, local copies, waits for them, and re-layouts, advance(): upper_cell = jnp.concatenate([centre[1:], zero_plane], 0)  40.2 us
    slice x11, local copies, waits for them, and re-layouts, with_halo(): lax.slice_in_dim(block, block.shape[dim] - width, None, axis=dim)  31.9 us
    ppermute x8, starting transfers between devices, with_halo(): lax.ppermute(lax.slice_in_dim(block, block.shape[dim] - width, None, axis...  29.2 us
    sub x1, other arithmetic, advance(): west_side + east_side + south_side + north_side + upper_cell + lower_cell  27.2 us
    add x1, other arithmetic, advance(): advect + jnp.maximum(courant_y, 0.0) * (centre - south_side)  23.8 us
  transfers between devices with their start and end apart: 17, of which 4 were waited for; matrix products, arithmetic and copies ran while one was open for 9% of the time, Pallas kernels for 0%

profile of v1, /device:TPU:1, one launch (start us, length us, event | category | flops | bytes accessed | tf_op | source)
XLA Modules:
  0.0 1101.8 jit_solution(3567088120577452072)
XLA Ops:
  6.5 16.5 %bitcast_multiply_fusion = f32[32,256,256]{2,0,1:T(8,128)S(1)} fusion(f32[1,32,256,256]{3,2,1,0:T(8,128)} %param.4, s32[32,256,256]{2,1,0:T(8,128)} %param.5), kind=kLoop, calls=%fused_computation.103 | loop fusion | flops 6291456 | bytes 25165824 | tf_op jit(solution)/shard_map/mul | solution.py:74
  23.0 6.0 collective-permute-start
  29.1 1.9 collective-permute-start.1
  31.0 4.8 collective-permute-done.1
  35.8 0.9 pad_maximum_fusion
  36.7 5.0 fusion.83
  41.7 3.7 copy.10
  45.4 3.5 collective-permute-start.2
  49.0 3.7 copy.12
  52.7 1.5 collective-permute-start.3
  54.2 13.4 %fusion.90 = (f32[31,256,256]{2,0,1:T(8,128)}, f32[31,256,256]{2,0,1:T(8,128)}) fusion(f32[32,256,256]{2,0,1:T(8,128)} %copy-done), kind=kLoop, calls=%fused_computation.136 | loop fusion | bytes 32505856 | tf_op jit(solution)/shard_map/slice | solution.py:48
  68.4 1.7 slice.205
  70.2 3.9 copy.11
  74.1 3.9 copy.13
  78.0 39.9 %fusion.59 = f32[32,256,256]{2,0,1:T(8,128)} fusion(f32[32,1,256]{2,0,1:T(8,128)S(1)} %collective-permute-done.1, f32[32,256,256]{2,0,1:T(8,128)} %copy-done, f32[32,1,256]{2,0,1:T(8,128)S(1)} %collective-permute-done, f32[31,256,256]{2,0,1:T(8,128)} %get-tuple-element.26, f32[1,256,256]{2,0,1:T(1,128)S(1)} %slice.205, ...), kind=kLoop, calls=%fused_computation.94 | loop fusion | flops 75497472 | bytes 41812496 | tf_op jit(solution)/shard_map/mul | solution.py:62
  117.9 0.8 fusion.89
  118.7 2.2 collective-permute-start.4
  120.9 2.1 collective-permute-start.5
  123.0 4.6 collective-permute-done.5
  127.6 4.0 pad_maximum_fusion.1
  131.6 4.8 fusion.82
  136.4 3.7 copy.14
  140.2 4.7 collective-permute-start.6
  144.8 3.7 copy.16
  148.6 1.3 collective-permute-start.7
  149.9 13.5 %fusion.88 = (f32[31,256,256]{2,0,1:T(8,128)}, f32[31,256,256]{2,0,1:T(8,128)}) fusion(f32[32,256,256]{2,0,1:T(8,128)} %fusion.59), kind=kLoop, calls=%fused_computation.134 | loop fusion | bytes 32505856 | tf_op jit(solution)/shard_map/slice | solution.py:48
  163.4 1.7 slice.212
  165.1 3.9 copy.15
  169.0 3.9 copy.17
  172.9 39.3 %fusion.41 = f32[32,256,256]{2,0,1:T(8,128)} fusion(f32[32,1,256]{2,0,1:T(8,128)S(1)} %collective-permute-done.5, f32[32,256,256]{2,0,1:T(8,128)} %fusion.59, f32[32,1,256]{2,0,1:T(8,128)S(1)} %collective-permute-done.4, f32[31,256,256]{2,0,1:T(8,128)} %get-tuple-element.22, f32[1,256,256]{2,0,1:T(1,128)S(1)} %slice.212, ...), kind=kLoop, calls=%fused_computation.68 | loop fusion | flops 75497472 | bytes 41812496 | tf_op jit(solution)/shard_map/mul | solution.py:62
  213.0 2.2 collective-permute-start.8
  215.2 2.3 collective-permute-start.9
  217.5 4.4 collective-permute-done.9
  221.9 4.0 pad_maximum_fusion.2
  225.9 4.8 fusion.81
  230.8 3.7 copy.18
  234.5 4.3 collective-permute-start.10
  238.8 3.7 copy.20
  242.5 1.3 collective-permute-start.11
  243.8 13.4 %fusion.86 = (f32[31,256,256]{2,0,1:T(8,128)}, f32[31,256,256]{2,0,1:T(8,128)}) fusion(f32[32,256,256]{2,0,1:T(8,128)} %fusion.41), kind=kLoop, calls=%fused_computation.132 | loop fusion | bytes 32505856 | tf_op jit(solution)/shard_map/slice | solution.py:48
  257.2 1.7 slice.219
  258.9 3.8 copy.19
  262.8 3.8 copy.21
  266.6 40.3 %fusion.23 = f32[32,256,256]{2,0,1:T(8,128)} fusion(f32[32,1,256]{2,0,1:T(8,128)S(1)} %collective-permute-done.9, f32[32,256,256]{2,0,1:T(8,128)} %fusion.41, f32[32,1,256]{2,0,1:T(8,128)S(1)} %collective-permute-done.8, f32[31,256,256]{2,0,1:T(8,128)} %get-tuple-element.18, f32[1,256,256]{2,0,1:T(1,128)S(1)} %slice.219, ...), kind=kLoop, calls=%fused_computation.42 | loop fusion | flops 75497472 | bytes 41812496 | tf_op jit(solution)/shard_map/mul | solution.py:62
  307.7 2.2 collective-permute-start.12
  309.9 2.7 collective-permute-start.13
  312.6 11.7 %fusion.67 = f32[32,256,256]{2,0,1:T(8,128)} fusion(s32[32,256,256]{2,1,0:T(8,128)} %param.5), kind=kLoop, calls=%fused_computation.105 | loop fusion | flops 4194304 | bytes 16777216 | tf_op jit(solution)/shard_map/convert_element_type | solution.py:71
  325.1 1.8 pad_maximum_fusion.3
  326.9 4.9 fusion.80
  331.8 3.7 copy.22
  335.5 4.2 collective-permute-start.14
  339.7 3.7 copy.24
  343.5 1.5 collective-permute-start.15
  345.0 13.5 %fusion.84 = (f32[31,256,256]{2,0,1:T(8,128)}, f32[31,256,256]{2,0,1:T(8,128)}) fusion(f32[32,256,256]{2,0,1:T(8,128)} %fusion.23), kind=kLoop, calls=%fused_computation.130 | loop fusion | bytes 32505856 | tf_op jit(solution)/shard_map/slice | solution.py:49
  358.5 1.7 slice.226
  360.3 3.8 copy.23
  364.0 3.9 copy.25
  368.0 23.8 %fusion.10 = f32[32,256,256]{2,0,1:T(8,128)} fusion(f32[32,256,256]{2,0,1:T(8,128)} %fusion.23, f32[32,1,256]{2,0,1:T(8,128)S(1)} %collective-permute-done.13, f32[32,1,256]{2,0,1:T(8,128)S(1)} %collective-permute-done.12, f32[32,258,1]{2,0,1:T(8,128)} %copy.23, f32[32,258,1]{2,0,1:T(8,128)} %copy.25, f32[]{:T(128)} %bitcast.4, f32[]{:T(128)} %bitcast.3, ...), kind=kLoop, calls=%fused_computation.21 | loop fusion | flops 39845888 | bytes 16908816 | tf_op jit(solution)/shard_map/add | solution.py:55
  391.8 27.2 %fusion.6 = f32[32,256,256]{2,0,1:T(8,128)} fusion(f32[32,1,256]{2,0,1:T(8,128)S(1)} %collective-permute-done.13, f32[32,256,256]{2,0,1:T(8,128)} %fusion.23, f32[32,1,256]{2,0,1:T(8,128)S(1)} %collective-permute-done.12, f32[31,256,256]{2,0,1:T(8,128)} %get-tuple-element.13, f32[1,256,256]{2,0,1:T(1,128)S(1)} %slice.226, ...), kind=kLoop, calls=%fused_computation.17 | loop fusion | flops 33554432 | bytes 33423872 | tf_op jit(solution)/shard_map/sub | solution.py:60
  419.0 11.5 %add_multiply_fusion = f32[16,256,256]{2,0,1:T(8,128)S(1)} fusion(f32[32,256,256]{2,0,1:T(8,128)} %fusion.67, f32[31,256,256]{2,0,1:T(8,128)} %get-tuple-element.14, f32[32,256,256]{2,0,1:T(8,128)} %fusion.6, f32[32,256,256]{2,0,1:T(8,128)} %fusion.10, f32[32,256,256]{2,0,1:T(8,128)S(1)} %bitcast.11, f32[32,256,256]{2,0,1:T(8,128)} %fusion.41, ...), kind=kLoop, calls=%fused_computation.124 | loop fusion | flops 19922944 | bytes 37486596 | tf_op jit(solution)/shard_map/mul | solution.py:80
  430.5 4.5 copy.26
  435.0 643.2 %all-gather.3.cloned.1.call-done = f32[128,256,256]{2,1,0:T(8,128)} async-done(((f32[16,256,256]{2,1,0:T(8,128)}), f32[128,256,256]{2,1,0:T(8,128)}) %all-gather.3.cloned.1.call-update) | async-done | bytes 33554448 | tf_op jit(solution)/shard_map/all_gather | solution.py:19
  1078.3 14.4 %reduce_sum.9 = f32[16,256,256]{2,1,0:T(8,128)} reduce(f32[8,16,256,256]{3,2,1,0:T(8,128)} %bitcast.14, f32[]{:T(128)} %constant.11.clone.1), dimensions={0}, to_apply=%region_0.0 | reduce | flops 7340032 | bytes 37748740 | tf_op jit(solution)/shard_map/reduce_sum | solution.py:19
  1092.6 1.9 constant_dynamic-slice_fusion
  (35 shorter events, 1.6 us)
Async XLA Ops:
  6.5 1071.7 %all-gather.3.cloned.1.call-start = ((), (), s32[]{:S(2)}) async-start(), calls=%async_computation | async-start | bytes 37748736 | tf_op jit(solution)/shard_map/all_gather | solution.py:19
  23.0 12.8 %copy-start = (f32[32,256,256]{2,0,1:T(8,128)}, f32[32,256,256]{2,0,1:T(8,128)S(1)}, u32[]{:S(2)}) copy-start(f32[32,256,256]{2,0,1:T(8,128)S(1)} %bitcast_multiply_fusion) | copy-start | bytes 25165828
  23.0 8.0 collective-permute-start
  29.1 6.7 collective-permute-start.1
  45.4 24.7 %collective-permute-start.2 = (f32[32,258,1]{1,0,2:T(8,128)S(1)}, f32[32,258,1]{1,0,2:T(8,128)S(1)}, u32[]{:S(2)}, u32[]{:S(2)}) collective-permute-start(f32[32,258,1]{1,0,2:T(8,128)S(1)} %copy.10), channel_id=1, source_target_pairs={{0,1},{1,2},{2,3},{4,5},{5,6},{6,7},{8,9},{9,10},{10,11},{12,13},{... | collective-permute-start | bytes 99080 | tf_op jit(solution)/shard_map/ppermute | solution.py:28
  52.7 21.4 %collective-permute-start.3 = (f32[32,258,1]{1,0,2:T(8,128)S(1)}, f32[32,258,1]{1,0,2:T(8,128)S(1)}, u32[]{:S(2)}, u32[]{:S(2)}) collective-permute-start(f32[32,258,1]{1,0,2:T(8,128)S(1)} %copy.12), channel_id=1, source_target_pairs={{1,0},{2,1},{3,2},{5,4},{6,5},{7,6},{9,8},{10,9},{11,10},{13,12},{... | collective-permute-start | bytes 99080 | tf_op jit(solution)/shard_map/ppermute | solution.py:31
  118.7 4.3 collective-permute-start.4
  120.9 6.7 collective-permute-start.5
  140.2 24.9 %collective-permute-start.6 = (f32[32,258,1]{1,0,2:T(8,128)S(1)}, f32[32,258,1]{1,0,2:T(8,128)S(1)}, u32[]{:S(2)}, u32[]{:S(2)}) collective-permute-start(f32[32,258,1]{1,0,2:T(8,128)S(1)} %copy.14), channel_id=1, source_target_pairs={{0,1},{1,2},{2,3},{4,5},{5,6},{6,7},{8,9},{9,10},{10,11},{12,13},{... | collective-permute-start | bytes 99080 | tf_op jit(solution)/shard_map/ppermute | solution.py:28
  148.6 20.4 %collective-permute-start.7 = (f32[32,258,1]{1,0,2:T(8,128)S(1)}, f32[32,258,1]{1,0,2:T(8,128)S(1)}, u32[]{:S(2)}, u32[]{:S(2)}) collective-permute-start(f32[32,258,1]{1,0,2:T(8,128)S(1)} %copy.16), channel_id=1, source_target_pairs={{1,0},{2,1},{3,2},{5,4},{6,5},{7,6},{9,8},{10,9},{11,10},{13,12},{... | collective-permute-start | bytes 99080 | tf_op jit(solution)/shard_map/ppermute | solution.py:31
  213.0 4.5 collective-permute-start.8
  215.2 6.7 collective-permute-start.9
  234.5 24.4 %collective-permute-start.10 = (f32[32,258,1]{1,0,2:T(8,128)S(1)}, f32[32,258,1]{1,0,2:T(8,128)S(1)}, u32[]{:S(2)}, u32[]{:S(2)}) collective-permute-start(f32[32,258,1]{1,0,2:T(8,128)S(1)} %copy.18), channel_id=1, source_target_pairs={{0,1},{1,2},{2,3},{4,5},{5,6},{6,7},{8,9},{9,10},{10,11},{12,13},{... | collective-permute-start | bytes 99080 | tf_op jit(solution)/shard_map/ppermute | solution.py:28
  242.5 20.2 %collective-permute-start.11 = (f32[32,258,1]{1,0,2:T(8,128)S(1)}, f32[32,258,1]{1,0,2:T(8,128)S(1)}, u32[]{:S(2)}, u32[]{:S(2)}) collective-permute-start(f32[32,258,1]{1,0,2:T(8,128)S(1)} %copy.20), channel_id=1, source_target_pairs={{1,0},{2,1},{3,2},{5,4},{6,5},{7,6},{9,8},{10,9},{11,10},{13,12},{... | collective-permute-start | bytes 99080 | tf_op jit(solution)/shard_map/ppermute | solution.py:31
  307.7 17.4 %collective-permute-start.12 = (f32[32,1,256]{2,0,1:T(8,128)S(1)}, f32[32,1,256]{2,0,1:T(8,128)S(1)}, u32[]{:S(2)}, u32[]{:S(2)}) collective-permute-start(f32[32,1,256]{2,0,1:T(8,128)S(1)} %get-tuple-element.15), channel_id=1, source_target_pairs={{0,4},{4,8},{8,12},{1,5},{5,9},{9,13},{2,6},{6,10},{10,14},{3,7},{... | collective-permute-start | bytes 98312 | tf_op jit(solution)/shard_map/ppermute | solution.py:28
  309.9 15.2 %slice-start = ((s8[8388608]{0:T(1024)(128)(4,1)}), s8[4194304]{0:T(1024)(128)(4,1)S(1)}, s32[]{:S(2)}) async-start(s8[8388608]{0:T(1024)(128)(4,1)} %bitcast.8), calls=%async_computation.1 | async-start | bytes 8388608
  309.9 15.2 %slice-start.1 = ((s8[8388608]{0:T(1024)(128)(4,1)}), s8[4194304]{0:T(1024)(128)(4,1)S(1)}, s32[]{:S(2)}) async-start(s8[8388608]{0:T(1024)(128)(4,1)} %bitcast.8), calls=%async_computation.2 | async-start | bytes 8388608
  309.9 15.2 %collective-permute-start.13 = (f32[32,1,256]{2,0,1:T(8,128)S(1)}, f32[32,1,256]{2,0,1:T(8,128)S(1)}, u32[]{:S(2)}, u32[]{:S(2)}) collective-permute-start(f32[32,1,256]{2,0,1:T(8,128)S(1)} %get-tuple-element.16), channel_id=1, source_target_pairs={{4,0},{8,4},{12,8},{5,1},{9,5},{13,9},{6,2},{10,6},{14,10},{7,3},{... | collective-permute-start | bytes 98312 | tf_op jit(solution)/shard_map/ppermute | solution.py:31
  335.5 24.7 %collective-permute-start.14 = (f32[32,258,1]{1,0,2:T(8,128)S(1)}, f32[32,258,1]{1,0,2:T(8,128)S(1)}, u32[]{:S(2)}, u32[]{:S(2)}) collective-permute-start(f32[32,258,1]{1,0,2:T(8,128)S(1)} %copy.22), channel_id=1, source_target_pairs={{0,1},{1,2},{2,3},{4,5},{5,6},{6,7},{8,9},{9,10},{10,11},{12,13},{... | collective-permute-start | bytes 99080 | tf_op jit(solution)/shard_map/ppermute | solution.py:28
  343.5 20.6 %collective-permute-start.15 = (f32[32,258,1]{1,0,2:T(8,128)S(1)}, f32[32,258,1]{1,0,2:T(8,128)S(1)}, u32[]{:S(2)}, u32[]{:S(2)}) collective-permute-start(f32[32,258,1]{1,0,2:T(8,128)S(1)} %copy.24), channel_id=1, source_target_pairs={{1,0},{2,1},{3,2},{5,4},{6,5},{7,6},{9,8},{10,9},{11,10},{13,12},{... | collective-permute-start | bytes 99080 | tf_op jit(solution)/shard_map/ppermute | solution.py:31
  364.0 27.7 %slice-start.4 = ((s8[4227072]{0:T(1024)(128)(4,1)}), s8[32768]{0:T(1024)(128)(4,1)S(1)}, s32[]{:S(2)}) async-start(s8[4227072]{0:T(1024)(128)(4,1)} %bitcast.12), calls=%async_computation.5 | async-start | bytes 65536
  368.0 23.8 %slice-start.5 = ((s8[4227072]{0:T(1024)(128)(4,1)}), s8[4194304]{0:T(1024)(128)(4,1)S(1)}, s32[]{:S(2)}) async-start(s8[4227072]{0:T(1024)(128)(4,1)} %bitcast.12), calls=%async_computation.6 | async-start | bytes 8388608
  368.0 51.0 %slice-start.2 = ((s8[8388608]{0:T(1024)(128)(4,1)}), s8[4194304]{0:T(1024)(128)(4,1)S(1)}, s32[]{:S(2)}) async-start(s8[8388608]{0:T(1024)(128)(4,1)} %bitcast.10), calls=%async_computation.3 | async-start | bytes 8388608
  391.8 27.2 %slice-start.3 = ((s8[8388608]{0:T(1024)(128)(4,1)}), s8[4194304]{0:T(1024)(128)(4,1)S(1)}, s32[]{:S(2)}) async-start(s8[8388608]{0:T(1024)(128)(4,1)} %bitcast.10), calls=%async_computation.4 | async-start | bytes 8388608
Sparse Core Ops, SparseCore 0:
  435.2 643.0 all-gather.2
